TPU v7x, 256 devices: a whole 4x4x8 slice. The times are simulated.
256 devices in a mesh: chan: 8 (over z_hi, x), tm: 16 (over z_lo, y), dp: 2 (over core).
Axes of the slice: x: 4, y: 4, z: 8 (z_hi: 2, z_lo: 4; z = z_hi * 4 + z_lo), core: 2. Of those that a mesh axis runs over, the one named last changes fastest.
Arguments:
- contexts: bfloat16 [512, 4, 16384], P('tm', 'dp', 'chan'), may hold values from -6 to 6
- cotangent: bfloat16 [512, 4, 16384], P('tm', 'dp', 'chan'), may hold values from -6 to 6
- w_in: bfloat16 [16384, 8192], P('chan', 'tm'), may hold values from -0.046875 to 0.046875
- w_out: bfloat16 [8192, 16384], P('tm', 'chan'), may hold values from -0.0625 to 0.0625
- time_weight: bfloat16 [512, 512], replicated, may hold values from -0.25 to 0.25
Outputs:
- grad_contexts: bfloat16 [512, 4, 16384], P('tm', 'dp', 'chan')
- grad_w_in: float32 [16384, 8192], P('chan', ('tm', 'dp'))
- grad_w_out: float32 [8192, 16384], P(('tm', 'dp'), 'chan')
- grad_time: float32 [512, 512], replicated
All inputs are finite; a program needn't handle non-finite values.
Results may differ from a plain program's by a relative error of at most 0.0057.
Values may be sent and summed in bfloat16 or wider, within the bound.
No kernel may reach another device: no remote copies, remote signals or barrier semaphores. Data moves between devices by JAX's collectives and lax.ppermute only.
A program may use at most 192 MiB of HBM per device.

v0:
```python
import functools
import math
import jax
import jax.numpy as jnp
from jax import lax
from jax.sharding import Mesh
from jax.sharding import PartitionSpec as P

TM = ("tz", "ty")
CHAN = ("zh", "cx")
tanh_scale = math.sqrt(2.0 / math.pi)
cubic_term = 0.044715


def gelu_pair(value):
    inner = jnp.tanh(tanh_scale * (value + cubic_term * value * value * value))
    result = 0.5 * value * (1.0 + inner)
    slope = 0.5 * (1.0 + inner) + 0.5 * value * (1.0 - inner * inner) * tanh_scale * (
        1.0 + 3.0 * cubic_term * value * value
    )
    return (result, slope)


def hidden_finish(hidden_pre, hidden_grad):
    act_hidden, slope_hidden = gelu_pair(hidden_pre)
    return (act_hidden.astype(jnp.bfloat16), (hidden_grad * slope_hidden).astype(jnp.bfloat16))


def gather_a2a(x, axis_name, size):
    b = jnp.broadcast_to(x[None], (size,) + x.shape)
    y = lax.all_to_all(b, axis_name, 0, 0, tiled=True)
    return y.reshape((size * x.shape[0],) + x.shape[1:])


def scatter_a2a(p, axis_name, size):
    y = lax.all_to_all(
        p.reshape((size, p.shape[0] // size) + p.shape[1:]), axis_name, 0, 0, tiled=True
    )
    return y.sum(0)


def on_device(contexts, cotangent, w_in, w_out, time_weight, tm, chan, chan_near, stages):
    local_len, batch_dev, width_dev = contexts.shape
    own = jnp.stack([contexts, cotangent]).transpose(0, 2, 1, 3)
    pair = lax.all_gather(own, TM, axis=2, tiled=True)
    whole_x, whole_dy = (pair[0], pair[1])
    length = whole_x.shape[1]
    pre_time = jnp.einsum("tl,blc->btc", time_weight, whole_x, preferred_element_type=jnp.float32)
    act_time, slope_time = gelu_pair(pre_time)
    mixed = (whole_x.astype(jnp.float32) + act_time).astype(jnp.bfloat16)
    rows = batch_dev * length
    mixed_rows = mixed.reshape(rows, width_dev)
    grad_rows = whole_dy.reshape(rows, width_dev)
    hidden_part = jnp.dot(mixed_rows, w_in, preferred_element_type=jnp.float32)
    hgrad_part = jnp.einsum("rc,hc->rh", grad_rows, w_out, preferred_element_type=jnp.float32)
    summed = scatter_a2a(jnp.stack([hidden_part, hgrad_part], 1), "cx", chan_near)
    summed = scatter_a2a(summed, "zh", chan // chan_near)
    act_rows, pre_grad_rows = hidden_finish(summed[:, 0], summed[:, 1])
    fin = gather_a2a(jnp.stack([act_rows, pre_grad_rows], 1), "zh", chan // chan_near)
    fin = gather_a2a(fin, "cx", chan_near)
    activation, pre_grad = (fin[:, 0], fin[:, 1])
    win_part = jnp.einsum("rc,rh->ch", mixed_rows, pre_grad, preferred_element_type=jnp.float32)
    wout_part = jnp.einsum("rh,rc->hc", activation, grad_rows, preferred_element_type=jnp.float32)
    grad_w_in, grad_w_out = (
        lax.psum_scatter(win_part, "dp", scatter_dimension=1, tiled=True),
        lax.psum_scatter(wout_part, "dp", scatter_dimension=0, tiled=True),
    )
    share = jnp.einsum(
        "rh,ch->rc", pre_grad, w_in, preferred_element_type=jnp.float32
    ) + grad_rows.astype(jnp.float32) * (1.0 / tm)
    share = share.reshape(batch_dev, length, width_dev)
    gate = (share * slope_time).astype(jnp.bfloat16)
    back = jnp.einsum("tl,btc->blc", time_weight, gate, preferred_element_type=jnp.float32)
    grad_own = lax.psum_scatter(share + back, TM, scatter_dimension=1, tiled=True)
    grad_contexts = grad_own.astype(jnp.bfloat16).transpose(1, 0, 2)
    time_part = jnp.einsum("btc,blc->tl", gate, whole_x, preferred_element_type=jnp.float32)
    for names, size in stages:
        time_part = scatter_a2a(time_part, names, size)
    for names, size in stages[::-1]:
        time_part = gather_a2a(time_part, names, size)
    grad_time = time_part
    return (grad_contexts, grad_w_in, grad_w_out, grad_time)


def solution(mesh):
    chan, tm, dp = (mesh.shape["chan"], mesh.shape["tm"], mesh.shape["dp"])
    far, near_z = (2, 4)
    fine = Mesh(
        mesh.devices.reshape(far, chan // far, near_z, tm // near_z, dp),
        ("zh", "cx", "tz", "ty", "dp"),
    )
    step = functools.partial(
        on_device,
        tm=tm,
        chan=chan,
        chan_near=chan // far,
        stages=((("dp",), dp), (("cx",), chan // far), (("zh",), far), (TM, tm)),
    )
    token = P(TM, "dp", CHAN)
    return jax.shard_map(
        step,
        mesh=fine,
        in_specs=(token, token, P(CHAN, TM), P(TM, CHAN), P()),
        out_specs=(token, P(CHAN, TM + ("dp",)), P(TM + ("dp",), CHAN), P()),
        check_vma=False,
    )
```

profile of v0, /device:TPU:1, one launch (start us, length us, event | category | flops | bytes accessed | tf_op | source)
XLA Modules:
  0.0 436.8 jit_solution(6076313547695591283)
XLA Ops:
  7.2 1.3 copy_bitcast_fusion
  8.6 0.8 maximum_bitcast_fusion
  9.4 0.0 reduce-scatter.4.cloned.1.call-start
  9.5 107.0 %all-gather.2.cloned.1.call-done = bf16[2,2,512,2048]{3,2,1,0:T(8,128)(2,1)} async-done(((bf16[2,2,32,2048]{3,2,1,0:T(8,128)(2,1)}), bf16[2,2,512,2048]{3,2,1,0:T(8,128)(2,1)}) %all-gather.2.cloned.1.call-update) | async-done | bytes 8388624 | tf_op jit(solution)/shard_map/all_gather | solution.py:45
  116.4 2.7 slice.25
  119.1 0.2 copy-done.9
  119.3 2.4 fusion.20
  121.7 1.7 slice-done.3
  123.5 6.5 %add_convert_fusion = (bf16[2,512,2048]{2,1,0:T(8,128)(2,1)S(1)}, f32[2,2048,512]{1,2,0:T(8,128)}) fusion(bf16[2,2,512,2048]{3,2,1,0:T(8,128)(2,1)S(1)} %bitcast.104, bf16[512,512]{1,0:T(8,128)(2,1)S(1)} %copy-done.7), kind=kOutput, calls=%fused_computation.12 | convolution fusion | flops 2170552320 | bytes 21495808 | tf_op jit(solution)/shard_map/tl,blc->btc/dot_general | solution.py:48
  130.0 2.3 fusion.17
  132.3 0.4 pad_maximum_fusion
  132.8 0.4 copy.61
  133.2 51.6 %all_to_all.60 = f32[4,256,2,512]{3,1,2,0:T(8,128)} all-to-all(f32[4,256,2,512]{3,1,2,0:T(8,128)S(1)} %copy.61), channel_id=1, replica_groups=mesh['zh'=2,'cx'=4,'tz'=4,'ty'=4,'dp'=2] {'cx'}, dimensions={0} | all-to-all | bytes 8388608 | tf_op jit(solution)/shard_map/all_to_all | solution.py:36
  184.9 2.8 reduce_sum.54
  187.6 0.1 copy.63
  187.7 21.7 %all_to_all.61 = f32[2,128,2,512]{3,1,2,0:T(8,128)S(1)} all-to-all(f32[2,128,2,512]{3,1,2,0:T(8,128)S(1)} %copy.63), channel_id=1, replica_groups=mesh['zh'=2,'cx'=4,'tz'=4,'ty'=4,'dp'=2] {'zh'}, dimensions={0} | all-to-all | bytes 2097152 | tf_op jit(solution)/shard_map/all_to_all | solution.py:36
  209.5 0.9 reduce_sum.55
  210.4 1.2 multiply_convert_fusion
  211.7 11.7 %all_to_all.62 = bf16[2,128,2,512]{3,1,2,0:T(8,128)(2,1)S(1)} all-to-all(bf16[2,128,2,512]{3,1,2,0:T(8,128)(2,1)S(1)} %broadcast_in_dim.40), channel_id=1, replica_groups=mesh['zh'=2,'cx'=4,'tz'=4,'ty'=4,'dp'=2] {'zh'}, dimensions={0} | all-to-all | bytes 1048576 | tf_op jit(solution)/shard_map/all_to_all | solution.py:31
  223.4 0.2 broadcast_in_dim.42
  223.6 18.1 %all_to_all.63 = bf16[4,256,2,512]{3,1,2,0:T(8,128)(2,1)S(1)} all-to-all(bf16[4,256,2,512]{3,1,2,0:T(8,128)(2,1)S(1)} %broadcast_in_dim.42), channel_id=1, replica_groups=mesh['zh'=2,'cx'=4,'tz'=4,'ty'=4,'dp'=2] {'cx'}, dimensions={0} | all-to-all | bytes 4194304 | tf_op jit(solution)/shard_map/all_to_all | solution.py:31
  241.7 0.1 copy.65
  241.9 2.4 multiply_add_fusion.1
  244.3 0.5 slice-done
  244.8 1.3 slice-done.1
  246.1 5.5 %fusion.6 = bf16[2,512,2048]{2,1,0:T(8,128)(2,1)S(1)} fusion(f32[2,512,2048]{2,1,0:T(8,128)S(1)} %bitcast.88, f32[2,2048,512]{1,2,0:T(8,128)S(1)} %bitcast.95), kind=kLoop, calls=%fused_computation.8 | loop fusion | flops 39845888 | bytes 20971520 | tf_op jit(solution)/shard_map/convert_element_type | solution.py:72
  251.6 1.9 copy-done.4
  253.5 6.0 %bitcast_add_fusion = f32[2,512,2048]{2,1,0:T(8,128)} fusion(f32[2,512,2048]{2,1,0:T(8,128)S(1)} %bitcast.89, bf16[2,512,2048]{2,1,0:T(8,128)(2,1)S(1)} %fusion.6, bf16[512,512]{1,0:T(8,128)(2,1)S(1)} %copy-done.8), kind=kOutput, calls=%fused_computation.9 | convolution fusion | flops 2149580800 | bytes 21495808 | tf_op jit(solution)/shard_map/tl,btc->blc/dot_general | solution.py:73
  259.5 0.0 reduce-scatter.6.cloned.1.call-start
  259.5 1.5 copy-done.6
  261.1 6.5 %fusion.27 = f32[2048,512]{1,0:T(8,128)} fusion(bf16[1024,2048]{1,0:T(8,128)(2,1)} %bitcast.109, bf16[1024,2,512]{2,0,1:T(8,128)(2,1)S(1)} %bitcast.97), kind=kOutput, calls=%fused_computation.30 | convolution fusion | flops 2147483648 | bytes 9437184 | tf_op jit(solution)/shard_map/rc,rh->ch/dot_general | solution.py:62
  267.6 0.3 reduce-scatter.8.cloned.1.call-start
  267.9 6.5 %fusion.26 = f32[512,2048]{1,0:T(8,128)} fusion(bf16[1024,2048]{1,0:T(8,128)(2,1)} %bitcast.91, bf16[1024,2,512]{2,0,1:T(8,128)(2,1)S(1)} %bitcast.98), kind=kOutput, calls=%fused_computation.28 | convolution fusion | flops 2147483648 | bytes 9437184 | tf_op jit(solution)/shard_map/rh,rc->hc/dot_general | solution.py:63
  274.5 5.8 %fusion.23 = f32[2,256,512]{2,1,0:T(8,128)S(1)} fusion(bf16[2,256,2,2048]{3,1,0,2:T(8,128)(2,1)} %bitcast.93, bf16[2,2,512,2048]{3,2,1,0:T(8,128)(2,1)} %all-gather.2.cloned.1.call-done), kind=kOutput, calls=%fused_computation.26 | convolution fusion | flops 2147483648 | bytes 9437184 | tf_op jit(solution)/shard_map/btc,blc->tl/dot_general | solution.py:76
  280.3 20.9 %all_to_all.64 = f32[2,256,512]{2,1,0:T(8,128)S(1)} all-to-all(f32[2,256,512]{2,1,0:T(8,128)S(1)} %fusion.23), channel_id=1, replica_groups=mesh['zh'=2,'cx'=4,'tz'=4,'ty'=4,'dp'=2] {'dp'}, dimensions={0} | all-to-all | bytes 2097152 | tf_op jit(solution)/shard_map/all_to_all | solution.py:36
  301.2 0.1 reduce_sum.56
  301.3 11.5 %all_to_all.65 = f32[4,64,512]{2,1,0:T(8,128)S(1)} all-to-all(f32[4,64,512]{2,1,0:T(8,128)S(1)} %bitcast.105), channel_id=1, replica_groups=mesh['zh'=2,'cx'=4,'tz'=4,'ty'=4,'dp'=2] {'cx'}, dimensions={0} | all-to-all | bytes 1048576 | tf_op jit(solution)/shard_map/all_to_all | solution.py:36
  312.8 11.3 %all_to_all.66 = f32[2,32,512]{2,1,0:T(8,128)S(1)} all-to-all(f32[2,32,512]{2,1,0:T(8,128)S(1)} %bitcast.107), channel_id=1, replica_groups=mesh['zh'=2,'cx'=4,'tz'=4,'ty'=4,'dp'=2] {'zh'}, dimensions={0} | all-to-all | bytes 262144 | tf_op jit(solution)/shard_map/all_to_all | solution.py:36
  324.2 43.5 %all_to_all.67 = f32[16,2,512]{2,1,0:T(2,128)S(1)} all-to-all(f32[16,2,512]{2,1,0:T(2,128)S(1)} %reshape.63), channel_id=1, replica_groups=mesh['zh'=2,'cx'=4,'tz'=4,'ty'=4,'dp'=2] {'tz','ty'}, dimensions={0} | all-to-all | bytes 131072 | tf_op jit(solution)/shard_map/all_to_all | solution.py:36
  367.8 26.0 %all_to_all.68 = f32[16,2,512]{2,1,0:T(2,128)S(1)} all-to-all(f32[16,2,512]{2,1,0:T(2,128)S(1)} %broadcast_in_dim.43), channel_id=1, replica_groups=mesh['zh'=2,'cx'=4,'tz'=4,'ty'=4,'dp'=2] {'tz','ty'}, dimensions={0} | all-to-all | bytes 131072 | tf_op jit(solution)/shard_map/all_to_all | solution.py:31
  393.8 11.3 %all_to_all.69 = f32[2,32,512]{2,1,0:T(8,128)S(1)} all-to-all(f32[2,32,512]{2,1,0:T(8,128)S(1)} %broadcast_in_dim.45), channel_id=1, replica_groups=mesh['zh'=2,'cx'=4,'tz'=4,'ty'=4,'dp'=2] {'zh'}, dimensions={0} | all-to-all | bytes 262144 | tf_op jit(solution)/shard_map/all_to_all | solution.py:31
  405.2 10.5 %all_to_all.70 = f32[4,64,512]{2,1,0:T(8,128)S(1)} all-to-all(f32[4,64,512]{2,1,0:T(8,128)S(1)} %broadcast_in_dim.47), channel_id=1, replica_groups=mesh['zh'=2,'cx'=4,'tz'=4,'ty'=4,'dp'=2] {'cx'}, dimensions={0} | all-to-all | bytes 1048576 | tf_op jit(solution)/shard_map/all_to_all | solution.py:31
  415.8 0.1 broadcast_in_dim.49
  415.9 9.2 %all_to_all.71 = f32[2,256,512]{2,1,0:T(8,128)S(1)} all-to-all(f32[2,256,512]{2,1,0:T(8,128)S(1)} %broadcast_in_dim.49), channel_id=1, replica_groups=mesh['zh'=2,'cx'=4,'tz'=4,'ty'=4,'dp'=2] {'dp'}, dimensions={0} | all-to-all | bytes 2097152 | tf_op jit(solution)/shard_map/all_to_all | solution.py:31
  425.1 1.2 convert_bitcast_fusion
  426.3 1.0 copy.69
  427.3 2.0 reduce-scatter.8.cloned.1.call-done
  429.3 1.0 copy.78
  (44 shorter events, 0.5 us)
Async XLA Ops:
  7.2 122.8 %copy-start = (bf16[2048,512]{1,0:T(8,128)(2,1)S(1)}, bf16[2048,512]{1,0:T(8,128)(2,1)}, u32[]{:S(2)}) copy-start(bf16[2048,512]{1,0:T(8,128)(2,1)} %param.7) | copy-start | bytes 6291460
  7.2 109.3 %all-gather.2.cloned.1.call-start = ((), (), s32[]{:S(2)}) async-start(), calls=%async_computation.15 | async-start | bytes 8912896 | tf_op jit(solution)/shard_map/all_gather | solution.py:45
  9.4 415.7 %reduce-scatter.4.cloned.1.call-start = ((), (), s32[]{:S(2)}) async-start(), calls=%async_computation.16 | async-start | bytes 8912896 | tf_op jit(solution)/shard_map/reduce_scatter | solution.py:74
  116.4 2.9 copy-start.9
  116.4 5.3 %slice-start.2 = ((s8[8388608]{0:T(1024)(128)(4,1)}), s8[4194304]{0:T(1024)(128)(4,1)S(1)}, s32[]{:S(2)}) async-start(s8[8388608]{0:T(1024)(128)(4,1)} %bitcast.103), calls=%async_computation.21 | async-start | bytes 8388608
  119.1 2.6 copy-start.2
  119.3 4.2 slice-start.3
  119.3 4.2 copy-start.7
  130.0 2.3 copy-start.10
  223.6 18.3 %copy-start.3 = (bf16[1,2,512,2048]{3,2,1,0:T(8,128)(2,1)S(1)}, bf16[1,2,512,2048]{3,2,1,0:T(8,128)(2,1)}, u32[]{:S(2)}) copy-start(bf16[1,2,512,2048]{3,2,1,0:T(8,128)(2,1)} %copy-done.2) | copy-start | bytes 12582916
  241.9 2.5 copy-start.5
  241.9 2.9 slice-start
  241.9 4.2 slice-start.1
  246.1 7.4 %copy-start.8 = (bf16[512,512]{1,0:T(8,128)(2,1)S(1)}, bf16[512,512]{1,0:T(8,128)(2,1)}, u32[]{:S(2)}) copy-start(bf16[512,512]{1,0:T(8,128)(2,1)} %param.9) | copy-start | bytes 1572868
  251.6 1.9 copy-start.4
  259.5 1.6 copy-start.6
  259.5 167.8 %reduce-scatter.6.cloned.1.call-start = ((), (), s32[]{:S(2)}) async-start(), calls=%async_computation.17 | async-start | bytes 6291456 | tf_op jit(solution)/shard_map/reduce_scatter | solution.py:65
  267.6 161.7 %reduce-scatter.8.cloned.1.call-start = ((), (), s32[]{:S(2)}) async-start(), calls=%async_computation.18 | async-start | bytes 6291456 | tf_op jit(solution)/shard_map/reduce_scatter | solution.py:66
  405.2 25.1 %copy-start.1 = (bf16[2048,512]{1,0:T(8,128)(2,1)S(1)}, bf16[2048,512]{1,0:T(8,128)(2,1)}, u32[]{:S(2)}) copy-start(bf16[2048,512]{1,0:T(8,128)(2,1)} %param.7) | copy-start | bytes 6291460
Sparse Core Ops, SparseCore 0:
  10.4 106.0 all-gather.1
  259.6 123.1 reduce-scatter.3
  385.9 21.5 reduce-scatter.5
  410.4 18.7 reduce-scatter.7
where the time goes:
time: 438 us; the launch traced here: 437 us
  blocking collectives  247 us (56%)
  waiting for transfers between devices  109 us (25%)
  matrix products  38.5 us (9%)
  local copies, waits for them, and re-layouts  14.3 us (3%)
  between operations  14 us (3%)
  other arithmetic  13.1 us (3%)
    all_to_all x6, blocking collectives, scatter_a2a(): lax.all_to_all(p.reshape((size, p.shape[0] // size) + p.shape[1:]), axis_...  161 us
    all_gather x1, waiting for transfers between devices, on_device(): pair = lax.all_gather(own, TM, axis=2, tiled=True)  107 us
    all_to_all x6, blocking collectives, gather_a2a(): y = lax.all_to_all(b, axis_name, 0, 0, tiled=True)  86.8 us
    unnamed x32, local copies, waits for them, and re-layouts  9.14 us
  transfers between devices with their start and end apart: 4, of which 2 were waited for; matrix products, arithmetic and copies ran while one was open for 5% of the time, Pallas kernels for 0%

commit v1 on v0

--- a/solution.py
+++ b/solution.py
@@ -42,7 +42,7 @@
 def on_device(contexts, cotangent, w_in, w_out, time_weight, tm, chan, chan_near, stages):
     local_len, batch_dev, width_dev = contexts.shape
     own = jnp.stack([contexts, cotangent]).transpose(0, 2, 1, 3)
-    pair = lax.all_gather(own, TM, axis=2, tiled=True)
+    pair = jnp.concatenate(lax.all_to_all(jnp.stack([own] * lax.axis_size(TM)), TM, 0, 0), axis=2)
     whole_x, whole_dy = (pair[0], pair[1])
     length = whole_x.shape[1]
     pre_time = jnp.einsum("tl,blc->btc", time_weight, whole_x, preferred_element_type=jnp.float32)

time: 438 us -> 524 us (1.20)
  blocking collectives: 247 us -> 440 us
  waiting for transfers between devices: 109 us -> 2.54 us
    all_to_all x0 -> x1, blocking collectives: none -> 191 us  [on_device(): lax.all_to_all(jnp.stack([own] * lax.axis_size(TM)), TM, 0, 0)]
    all_gather x1 -> x0, waiting for transfers between devices: 107 us -> none  [on_device(): pair = lax.all_gather(own, TM, axis=2, tiled=True)]
  transfers between devices with their start and end apart: 4 -> 3, of which waited for: 2 -> 1; matrix products, arithmetic and copies ran while one was open for 5% -> 4% of each run, Pallas kernels for 0% -> 0%
where the time goes in v1:
time: 524 us
  blocking collectives  440 us (84%)
  matrix products  38.5 us (7%)
  local copies, waits for them, and re-layouts  14.4 us (3%)
  other arithmetic  14.1 us (3%)
  between operations  14.1 us (3%)
    all_to_all x1, blocking collectives, on_device(): lax.all_to_all(jnp.stack([own] * lax.axis_size(TM)), TM, 0, 0)  191 us
    all_to_all x6, blocking collectives, scatter_a2a(): lax.all_to_all(p.reshape((size, p.shape[0] // size) + p.shape[1:]), axis_...  157 us
    all_to_all x6, blocking collectives, gather_a2a(): y = lax.all_to_all(b, axis_name, 0, 0, tiled=True)  91.4 us
  transfers between devices with their start and end apart: 3, of which 1 were waited for; matrix products, arithmetic and copies ran while one was open for 4% of the time, Pallas kernels for 0%

profile of v1, /device:TPU:1, one launch (start us, length us, event | category | flops | bytes accessed | tf_op | source)
XLA Modules:
  0.0 523.7 jit_solution(6539046584726120981)
XLA Ops:
  7.2 2.0 maximum_bitcast_fusion
  9.2 0.2 copy.65
  9.3 1.1 stack.15
  10.4 191.2 %all_to_all.65 = bf16[16,2,2,32,2048]{4,3,2,1,0:T(8,128)(2,1)S(1)} all-to-all(bf16[16,2,2,32,2048]{4,3,2,1,0:T(8,128)(2,1)S(1)} %stack.15), channel_id=1, replica_groups=mesh['zh'=2,'cx'=4,'tz'=4,'ty'=4,'dp'=2] {'tz','ty'}, dimensions={0} | all-to-all | bytes 16777216 | tf_op jit(solution)/shard_map/all_to_all | solution.py:45
  201.6 1.2 fusion.29
  202.8 0.6 copy.66
  203.4 0.6 copy.67
  204.0 2.5 copy-done.10
  206.4 2.4 fusion.14
  208.8 6.6 %add_convert_fusion = (bf16[2,512,2048]{2,1,0:T(8,128)(2,1)S(1)}, f32[2,2048,512]{1,2,0:T(8,128)}) fusion(bf16[2,512,2048]{2,1,0:T(8,128)(2,1)S(1)} %bitcast.93, bf16[512,512]{1,0:T(8,128)(2,1)S(1)} %copy-done.8), kind=kOutput, calls=%fused_computation.12 | convolution fusion | flops 2170552320 | bytes 17301504 | tf_op jit(solution)/shard_map/tl,blc->btc/dot_general | solution.py:48
  215.4 2.3 fusion.11
  217.7 0.4 pad_maximum_fusion
  218.2 0.4 copy.68
  218.6 49.7 %all_to_all.66 = f32[4,256,2,512]{3,1,2,0:T(8,128)} all-to-all(f32[4,256,2,512]{3,1,2,0:T(8,128)S(1)} %copy.68), channel_id=1, replica_groups=mesh['zh'=2,'cx'=4,'tz'=4,'ty'=4,'dp'=2] {'cx'}, dimensions={0} | all-to-all | bytes 8388608 | tf_op jit(solution)/shard_map/all_to_all | solution.py:36
  268.3 2.8 reduce_sum.54
  271.1 0.1 copy.70
  271.2 18.8 %all_to_all.67 = f32[2,128,2,512]{3,1,2,0:T(8,128)S(1)} all-to-all(f32[2,128,2,512]{3,1,2,0:T(8,128)S(1)} %copy.70), channel_id=1, replica_groups=mesh['zh'=2,'cx'=4,'tz'=4,'ty'=4,'dp'=2] {'zh'}, dimensions={0} | all-to-all | bytes 2097152 | tf_op jit(solution)/shard_map/all_to_all | solution.py:36
  290.0 0.9 reduce_sum.55
  290.9 1.2 multiply_convert_fusion
  292.2 16.1 %all_to_all.68 = bf16[2,128,2,512]{3,1,2,0:T(8,128)(2,1)S(1)} all-to-all(bf16[2,128,2,512]{3,1,2,0:T(8,128)(2,1)S(1)} %broadcast_in_dim.40), channel_id=1, replica_groups=mesh['zh'=2,'cx'=4,'tz'=4,'ty'=4,'dp'=2] {'zh'}, dimensions={0} | all-to-all | bytes 1048576 | tf_op jit(solution)/shard_map/all_to_all | solution.py:31
  308.4 0.2 broadcast_in_dim.42
  308.6 18.1 %all_to_all.69 = bf16[4,256,2,512]{3,1,2,0:T(8,128)(2,1)S(1)} all-to-all(bf16[4,256,2,512]{3,1,2,0:T(8,128)(2,1)S(1)} %broadcast_in_dim.42), channel_id=1, replica_groups=mesh['zh'=2,'cx'=4,'tz'=4,'ty'=4,'dp'=2] {'cx'}, dimensions={0} | all-to-all | bytes 4194304 | tf_op jit(solution)/shard_map/all_to_all | solution.py:31
  326.6 0.1 copy.72
  326.8 2.4 multiply_add_fusion.1
  329.3 0.5 slice-done
  329.7 1.3 slice-done.1
  331.0 5.5 %fusion.6 = bf16[2,512,2048]{2,1,0:T(8,128)(2,1)S(1)} fusion(f32[2,512,2048]{2,1,0:T(8,128)S(1)} %bitcast.82, f32[2,2048,512]{1,2,0:T(8,128)S(1)} %bitcast.89), kind=kLoop, calls=%fused_computation.8 | loop fusion | flops 39845888 | bytes 20971520 | tf_op jit(solution)/shard_map/convert_element_type | solution.py:72
  336.5 1.9 copy-done.4
  338.5 6.0 %bitcast_add_fusion = f32[2,512,2048]{2,1,0:T(8,128)} fusion(f32[2,512,2048]{2,1,0:T(8,128)S(1)} %bitcast.83, bf16[2,512,2048]{2,1,0:T(8,128)(2,1)S(1)} %fusion.6, bf16[512,512]{1,0:T(8,128)(2,1)S(1)} %copy-done.9), kind=kOutput, calls=%fused_computation.9 | convolution fusion | flops 2149580800 | bytes 21495808 | tf_op jit(solution)/shard_map/tl,btc->blc/dot_general | solution.py:73
  344.5 1.5 copy-done.6
  346.0 6.5 %fusion.18 = f32[2048,512]{1,0:T(8,128)} fusion(bf16[1024,2048]{1,0:T(8,128)(2,1)} %bitcast.105, bf16[1024,2,512]{2,0,1:T(8,128)(2,1)S(1)} %bitcast.91), kind=kOutput, calls=%fused_computation.24 | convolution fusion | flops 2147483648 | bytes 9437184 | tf_op jit(solution)/shard_map/rc,rh->ch/dot_general | solution.py:62
  352.5 0.3 reduce-scatter.8.cloned.1.call-start
  352.8 6.5 %fusion.17 = f32[512,2048]{1,0:T(8,128)} fusion(bf16[1024,2048]{1,0:T(8,128)(2,1)} %bitcast.85, bf16[1024,2,512]{2,0,1:T(8,128)(2,1)S(1)} %bitcast.92), kind=kOutput, calls=%fused_computation.22 | convolution fusion | flops 2147483648 | bytes 9437184 | tf_op jit(solution)/shard_map/rh,rc->hc/dot_general | solution.py:63
  359.3 5.8 %convolution_bitcast_fusion = f32[2,256,512]{2,1,0:T(8,128)S(1)} fusion(bf16[2,256,2,2048]{3,1,0,2:T(8,128)(2,1)} %bitcast.87, bf16[2,512,2048,1]{2,1,3,0:T(8,128)(2,1)} %bitcast.94), kind=kOutput, calls=%fused_computation.20 | convolution fusion | flops 2147483648 | bytes 9437184 | tf_op jit(solution)/shard_map/btc,blc->tl/dot_general | solution.py:76
  365.2 23.1 %all_to_all.70 = f32[2,256,512]{2,1,0:T(8,128)S(1)} all-to-all(f32[2,256,512]{2,1,0:T(8,128)S(1)} %convolution_bitcast_fusion), channel_id=1, replica_groups=mesh['zh'=2,'cx'=4,'tz'=4,'ty'=4,'dp'=2] {'dp'}, dimensions={0} | all-to-all | bytes 2097152 | tf_op jit(solution)/shard_map/all_to_all | solution.py:36
  388.2 0.1 reduce_sum.56
  388.3 11.4 %all_to_all.71 = f32[4,64,512]{2,1,0:T(8,128)S(1)} all-to-all(f32[4,64,512]{2,1,0:T(8,128)S(1)} %bitcast.99), channel_id=1, replica_groups=mesh['zh'=2,'cx'=4,'tz'=4,'ty'=4,'dp'=2] {'cx'}, dimensions={0} | all-to-all | bytes 1048576 | tf_op jit(solution)/shard_map/all_to_all | solution.py:36
  399.8 11.3 %all_to_all.72 = f32[2,32,512]{2,1,0:T(8,128)S(1)} all-to-all(f32[2,32,512]{2,1,0:T(8,128)S(1)} %bitcast.101), channel_id=1, replica_groups=mesh['zh'=2,'cx'=4,'tz'=4,'ty'=4,'dp'=2] {'zh'}, dimensions={0} | all-to-all | bytes 262144 | tf_op jit(solution)/shard_map/all_to_all | solution.py:36
  411.1 42.9 %all_to_all.73 = f32[16,2,512]{2,1,0:T(2,128)S(1)} all-to-all(f32[16,2,512]{2,1,0:T(2,128)S(1)} %reshape.74), channel_id=1, replica_groups=mesh['zh'=2,'cx'=4,'tz'=4,'ty'=4,'dp'=2] {'tz','ty'}, dimensions={0} | all-to-all | bytes 131072 | tf_op jit(solution)/shard_map/all_to_all | solution.py:36
  454.1 18.8 %all_to_all.74 = f32[16,2,512]{2,1,0:T(2,128)S(1)} all-to-all(f32[16,2,512]{2,1,0:T(2,128)S(1)} %broadcast_in_dim.43), channel_id=1, replica_groups=mesh['zh'=2,'cx'=4,'tz'=4,'ty'=4,'dp'=2] {'tz','ty'}, dimensions={0} | all-to-all | bytes 131072 | tf_op jit(solution)/shard_map/all_to_all | solution.py:31
  472.9 18.1 %all_to_all.75 = f32[2,32,512]{2,1,0:T(8,128)S(1)} all-to-all(f32[2,32,512]{2,1,0:T(8,128)S(1)} %broadcast_in_dim.45), channel_id=1, replica_groups=mesh['zh'=2,'cx'=4,'tz'=4,'ty'=4,'dp'=2] {'zh'}, dimensions={0} | all-to-all | bytes 262144 | tf_op jit(solution)/shard_map/all_to_all | solution.py:31
  491.1 9.6 %all_to_all.76 = f32[4,64,512]{2,1,0:T(8,128)S(1)} all-to-all(f32[4,64,512]{2,1,0:T(8,128)S(1)} %broadcast_in_dim.47), channel_id=1, replica_groups=mesh['zh'=2,'cx'=4,'tz'=4,'ty'=4,'dp'=2] {'cx'}, dimensions={0} | all-to-all | bytes 1048576 | tf_op jit(solution)/shard_map/all_to_all | solution.py:31
  500.7 0.1 broadcast_in_dim.49
  500.9 10.7 %all_to_all.77 = f32[2,256,512]{2,1,0:T(8,128)S(1)} all-to-all(f32[2,256,512]{2,1,0:T(8,128)S(1)} %broadcast_in_dim.49), channel_id=1, replica_groups=mesh['zh'=2,'cx'=4,'tz'=4,'ty'=4,'dp'=2] {'dp'}, dimensions={0} | all-to-all | bytes 2097152 | tf_op jit(solution)/shard_map/all_to_all | solution.py:31
  511.5 1.1 convert_bitcast_fusion
  512.7 1.0 copy.77
  513.7 2.5 reduce-scatter.8.cloned.1.call-done
  516.1 1.0 copy.84
  (42 shorter events, 0.5 us)
Async XLA Ops:
  7.2 208.2 %copy-start = (bf16[2048,512]{1,0:T(8,128)(2,1)S(1)}, bf16[2048,512]{1,0:T(8,128)(2,1)}, u32[]{:S(2)}) copy-start(bf16[2048,512]{1,0:T(8,128)(2,1)} %param.7) | copy-start | bytes 6291460
  7.2 504.4 %reduce-scatter.4.cloned.1.call-start = ((), (), s32[]{:S(2)}) async-start(), calls=%async_computation.16 | async-start | bytes 8912896 | tf_op jit(solution)/shard_map/reduce_scatter | solution.py:74
  203.3 5.4 %copy-start.7 = (bf16[1,2,16,32,2048]{4,3,2,1,0:T(8,128)(2,1)}, bf16[1,2,16,32,2048]{4,3,2,1,0:T(8,128)(2,1)S(1)}, u32[]{:S(2)}) copy-start(bf16[1,2,16,32,2048]{4,3,2,1,0:T(8,128)(2,1)S(1)} %copy.66) | copy-start | bytes 12582916
  203.4 3.1 copy-start.10
  203.9 4.8 copy-start.2
  206.4 2.4 copy-start.8
  215.4 2.3 copy-start.11
  308.5 18.3 %copy-start.3 = (bf16[1,2,16,32,2048]{4,3,2,1,0:T(8,128)(2,1)S(1)}, bf16[1,2,16,32,2048]{4,3,2,1,0:T(8,128)(2,1)}, u32[]{:S(2)}) copy-start(bf16[1,2,16,32,2048]{4,3,2,1,0:T(8,128)(2,1)} %copy-done.2) | copy-start | bytes 12582916
  326.8 2.5 copy-start.5
  326.8 2.9 slice-start
  326.8 4.2 slice-start.1
  331.0 7.4 %copy-start.9 = (bf16[512,512]{1,0:T(8,128)(2,1)S(1)}, bf16[512,512]{1,0:T(8,128)(2,1)}, u32[]{:S(2)}) copy-start(bf16[512,512]{1,0:T(8,128)(2,1)} %param.9) | copy-start | bytes 1572868
  336.5 2.0 copy-start.4
  344.4 1.6 copy-start.6
  344.4 169.2 %reduce-scatter.6.cloned.1.call-start = ((), (), s32[]{:S(2)}) async-start(), calls=%async_computation.17 | async-start | bytes 6291456 | tf_op jit(solution)/shard_map/reduce_scatter | solution.py:65
  352.5 163.6 %reduce-scatter.8.cloned.1.call-start = ((), (), s32[]{:S(2)}) async-start(), calls=%async_computation.18 | async-start | bytes 6291456 | tf_op jit(solution)/shard_map/reduce_scatter | solution.py:66
  491.1 26.1 %copy-start.1 = (bf16[2048,512]{1,0:T(8,128)(2,1)S(1)}, bf16[2048,512]{1,0:T(8,128)(2,1)}, u32[]{:S(2)}) copy-start(bf16[2048,512]{1,0:T(8,128)(2,1)} %param.7) | copy-start | bytes 6291460
Sparse Core Ops, SparseCore 0:
  344.6 124.7 reduce-scatter.3
  472.5 21.8 reduce-scatter.5
  497.5 18.6 reduce-scatter.7
